TPU v7x, 256 devices: a whole 4x4x8 slice. The times are simulated.
256 devices in a mesh: blk: 64 (over z_hi, x, y, core), path: 4 (over z_lo).
Axes of the slice: x: 4, y: 4, z: 8 (z_hi: 2, z_lo: 4; z = z_hi * 4 + z_lo), core: 2. Of those that a mesh axis runs over, the one named last changes fastest.
Arguments:
- records: bfloat16 [65536, 512], P('blk'), may hold values from -87.98545 to 87.98545
- coefficients: float32 [65536, 64], P('blk', 'path'), may hold values from -6 to 6
- velocity: float32 [65536, 64], P('blk', 'path'), may hold values from -3 to 3
- targets: float32 [65536, 64], P('blk', 'path'), may hold values from -6 to 6
- block_local: int32 [3, 1536], P(None, 'blk'), may hold values from 0 to 1023
- block_count: int32 [3, 64], replicated, may hold values from 1 to 24, 1024 in all within a row
- candidates: bfloat16 [32768, 512], P('blk'), may hold values from -87.98545 to 87.98545
- frequencies: bfloat16 [512, 1024], replicated, may hold values from -0.25 to 0.25
- phases: float32 [1024], replicated, may hold values from -3.140625 to 3.140625
- prior_weight: float32 [1024, 64], P(None, 'path'), may hold values from -6 to 6
Outputs:
- coefficients_out: float32 [65536, 64], P('blk', 'path')
- velocity_out: float32 [65536, 64], P('blk', 'path')
- scores: float32 [32768, 64], P('blk', 'path')
- path_rms: float32 [32768], P('blk')
Inputs may be any that keep to these rules, and one draw needn't show every extreme that they name: `block_count`: each row sums to 1024, and its largest entry is exactly 24. `block_local`: index within the owner's records; a slot at or beyond the owner's count in that step is not used. Used entries of one owner may repeat.
All inputs are finite; a program needn't handle non-finite values.
Results may differ from a plain program's by a relative error of at most 0.0014.
Values may be sent and summed in bfloat16 or wider, within the bound.
No kernel may reach another device: no remote copies, remote signals or barrier semaphores. Data moves between devices by JAX's collectives and lax.ppermute only.
A program may use at most 128 MiB of HBM per device.

v0:
```python
import math
import jax
import jax.numpy as jnp
from jax import lax
from jax.sharding import PartitionSpec as P

NOISE = 0.5
MOMENTUM = 0.9
RATE = 0.3
EPSILON = 1e-06
SIGNAL = 9.0


def passed_along(shard, axis, by):
    length = lax.axis_size(axis)
    return lax.ppermute(shard, axis, [(i, (i + by) % length) for i in range(length)])


def square_norms(row_block):
    widened = row_block.astype(jnp.float32)
    return jnp.sum(widened * widened, axis=1)


def kernel_apply(left_rows, left_norms, right_rows, right_norms, weights):
    dot_values = lax.dot_general(
        left_rows, right_rows, (((1,), (1,)), ((), ())), preferred_element_type=jnp.float32
    )
    distance = left_norms[:, None] + right_norms[None, :] - 2.0 * dot_values
    kernel_tile = SIGNAL * jnp.exp(-distance / left_rows.shape[1])
    return jnp.dot(kernel_tile, weights, precision=lax.Precision.HIGHEST)


def prior_values(cand_rows, frequencies, phases, prior_weight):
    angles = (
        jnp.dot(cand_rows, frequencies, preferred_element_type=jnp.float32) * math.sqrt(2.0)
        + phases[None, :]
    )
    features = math.sqrt(2.0 * SIGNAL / frequencies.shape[1]) * jnp.cos(angles)
    return jnp.dot(features, prior_weight, precision=lax.Precision.HIGHEST)


def shards(
    records,
    coefficients,
    velocity,
    targets,
    block_local,
    block_count,
    candidates,
    frequencies,
    phases,
    prior_weight,
):
    record_total = records.shape[0] * lax.axis_size("blk")
    root_count = jnp.sqrt(jnp.float32(record_total))
    slot_count = block_local.shape[1]
    own_index = lax.axis_index("blk")
    neighbour = passed_along(candidates, "blk", 1)
    work_norms = square_norms(records)
    slot_ids = jnp.arange(slot_count, dtype=jnp.int32)
    for repeat in range(block_local.shape[0]):
        local_rows = block_local[repeat]
        own_count = lax.dynamic_index_in_dim(block_count[repeat], own_index, 0, keepdims=False)
        is_live = slot_ids < own_count
        gathered = lax.all_gather(records[local_rows], "blk", axis=0, tiled=True)
        gathered_norms = square_norms(gathered)
        work_coefs = coefficients
        whole_sum = lax.psum(
            kernel_apply(gathered, gathered_norms, records, work_norms, work_coefs), "blk"
        )
        product = lax.dynamic_slice_in_dim(whole_sum, own_index * slot_count, slot_count, 0)
        product = product / root_count
        gradient = jnp.where(
            is_live[:, None], product + NOISE * coefficients[local_rows] - targets[local_rows], 0.0
        )
        velocity = (MOMENTUM * velocity).at[local_rows].add(-RATE * gradient)
        coefficients = coefficients + velocity
    own_sum = kernel_apply(candidates, square_norms(candidates), records, work_norms, coefficients)
    next_sum = kernel_apply(neighbour, square_norms(neighbour), records, work_norms, coefficients)
    own_sum, next_sum = (own_sum, next_sum)
    first_part = prior_values(candidates, frequencies, phases, prior_weight) + own_sum / root_count
    next_term = next_sum / root_count
    passed = passed_along(first_part, "blk", 1)
    scores = passed_along(passed + next_term, "blk", 1)
    squares_local = jnp.sum(scores * scores, axis=1)
    summed = lax.psum(squares_local, "path")
    path_rms = jnp.sqrt(summed / (scores.shape[1] * lax.axis_size("path")) + EPSILON)
    return (coefficients, velocity, scores, path_rms)


def solution(mesh):
    return jax.shard_map(
        shards,
        mesh=mesh,
        in_specs=(
            P("blk", None),
            P("blk", "path"),
            P("blk", "path"),
            P("blk", "path"),
            P(None, "blk"),
            P(),
            P("blk", None),
            P(),
            P(),
            P(None, "path"),
        ),
        out_specs=(P("blk", "path"), P("blk", "path"), P("blk", "path"), P("blk")),
        check_vma=False,
    )
```

profile of v0, /device:TPU:0, one launch (start us, length us, event | category | flops | bytes accessed | tf_op | source)
XLA Modules:
  0.0 2484.4 jit_solution(10862809576927528547)
XLA Ops:
  7.3 0.9 fusion.87
  8.2 2.6 gather_fusion
  10.8 2.6 gather_fusion.3
  13.5 2.6 gather_fusion.6
  16.2 1.0 copy.32
  19.1 1.0 copy.36
  20.8 1.0 copy.34
  22.5 0.7 constant_dynamic-slice_fusion
  23.2 0.6 iota_compare_fusion.2
  23.8 0.6 iota_compare_fusion.1
  24.5 0.6 iota_compare_fusion
  25.6 2.1 fusion.110
  27.7 2.0 fusion.109
  29.7 64.4 %all-gather.7.cloned.1.call-done = bf16[1536,512]{1,0:T(8,128)(2,1)} async-done(((bf16[24,512]{1,0:T(8,128)(2,1)}), bf16[1536,512]{1,0:T(8,128)(2,1)}) %all-gather.7.cloned.1.call-update) | async-done | bytes 1572880 | tf_op jit(solution)/shard_map/all_gather | solution.py:65
  94.1 1.8 multiply_reduce_fusion.2
  95.9 3.3 fusion.106
  99.2 7.4 fusion.16
  107.0 65.2 %all-gather.9.cloned.1.call-done = bf16[1536,512]{1,0:T(8,128)(2,1)} async-done(((bf16[24,512]{1,0:T(8,128)(2,1)}), bf16[1536,512]{1,0:T(8,128)(2,1)}) %all-gather.9.cloned.1.call-update) | async-done | bytes 1572880 | tf_op jit(solution)/shard_map/all_gather | solution.py:65
  172.2 5.9 fusion.107
  178.1 72.2 %all-gather.11.cloned.1.call-done = bf16[1536,512]{1,0:T(8,128)(2,1)} async-done(((bf16[24,512]{1,0:T(8,128)(2,1)}), bf16[1536,512]{1,0:T(8,128)(2,1)}) %all-gather.11.cloned.1.call-update) | async-done | bytes 1572880 | tf_op jit(solution)/shard_map/all_gather | solution.py:65
  250.3 6.0 fusion.108
  256.7 707.5 %all-reduce.4.cloned.1.call-done = f32[1536,16]{0,1:T(8,128)} async-done(((f32[1536,16]{0,1:T(8,128)}), f32[1536,16]{0,1:T(8,128)}) %all-reduce.4.cloned.1.call-update) | async-done | bytes 98320 | tf_op jit(solution)/shard_map/psum | solution.py:68
  964.2 0.8 select_multiply_fusion.2
  965.1 0.9 scatter_fusion
  966.0 0.9 broadcast_multiply_fusion
  966.9 0.8 copy-done.5
  967.7 10.3 fusion.8
  978.1 1.8 multiply_reduce_fusion
  979.9 1.6 gather_fusion.4
  981.5 711.6 %all-reduce.6.cloned.1.call-done = f32[1536,16]{0,1:T(8,128)} async-done(((f32[1536,16]{0,1:T(8,128)}), f32[1536,16]{0,1:T(8,128)}) %all-reduce.6.cloned.1.call-update) | async-done | bytes 98320 | tf_op jit(solution)/shard_map/psum | solution.py:68
  1693.2 0.8 select_multiply_fusion.1
  1694.0 3.0 scatter_fusion.1
  1697.0 1.3 broadcast_multiply_fusion.1
  1698.3 10.2 fusion
  1708.5 3.1 fusion.111
  1712.3 711.4 %all-reduce.8.cloned.1.call-done = f32[1536,16]{0,1:T(8,128)} async-done(((f32[1536,16]{0,1:T(8,128)}), f32[1536,16]{0,1:T(8,128)}) %all-reduce.8.cloned.1.call-update) | async-done | bytes 98320 | tf_op jit(solution)/shard_map/psum | solution.py:68
  2423.7 0.8 select_multiply_fusion
  2424.6 0.9 scatter_fusion.2
  2425.6 4.1 fusion.63
  2429.7 9.1 fusion.60
  2439.2 1.2 multiply_reduce_fusion.4
  2440.4 10.3 collective-permute-done
  2450.7 2.4 fusion.69
  2453.2 0.8 copy.45
  2454.0 0.8 copy.46
  2454.8 9.9 collective-permute-done.2
  2464.7 11.5 psum.31
  2476.8 0.6 copy.54
  (67 shorter events, 6.7 us)
Async XLA Ops:
  7.2 20.5 copy-start
  7.2 18.1 copy-start.1
  7.2 17.9 copy-start.3
  7.2 13.6 copy-start.10
  7.2 14.7 copy-start.12
  7.2 86.9 %all-gather.7.cloned.1.call-start = ((), (), s32[]{:S(2)}) async-start(), calls=%async_computation.3 | async-start | bytes 1597440 | tf_op jit(solution)/shard_map/all_gather | solution.py:65
  10.8 161.4 %all-gather.9.cloned.1.call-start = ((), (), s32[]{:S(2)}) async-start(), calls=%async_computation.4 | async-start | bytes 1597440 | tf_op jit(solution)/shard_map/all_gather | solution.py:65
  13.4 236.9 %all-gather.11.cloned.1.call-start = ((), (), s32[]{:S(2)}) async-start(), calls=%async_computation.5 | async-start | bytes 1597440 | tf_op jit(solution)/shard_map/all_gather | solution.py:65
  16.1 948.1 %all-reduce.4.cloned.1.call-start = ((), (), s32[]{:S(2)}) async-start(), calls=%async_computation | async-start | bytes 196608 | tf_op jit(solution)/shard_map/psum | solution.py:68
  16.1 1692.4 %collective-permute-start.1 = (bf16[512,512]{1,0:T(8,128)(2,1)}, bf16[512,512]{1,0:T(8,128)(2,1)}, u32[]{:S(2)}, u32[]{:S(2)}) collective-permute-start(bf16[512,512]{1,0:T(8,128)(2,1)} %param.16), channel_id=1, source_target_pairs={{0,4},{4,8},{8,12},{12,16},{16,20},{20,24},{24,28},{28,32},{32,36}... | collective-permute-start | bytes 1572872 | tf_op jit(solution)/shard_map/ppermute | solution.py:16
  95.9 3.3 copy-start.8
  106.7 1586.5 %all-reduce.6.cloned.1.call-start = ((), (), s32[]{:S(2)}) async-start(), calls=%async_computation.1 | async-start | bytes 196608 | tf_op jit(solution)/shard_map/psum | solution.py:68
  178.1 787.0 %copy-start.4 = (f32[1024,16]{1,0:T(8,128)S(1)}, f32[1024,16]{1,0:T(8,128)}, u32[]{:S(2)}) copy-start(f32[1024,16]{1,0:T(8,128)} %copy.34) | copy-start | bytes 196612
  250.3 6.0 copy-start.7
  966.9 0.8 copy-start.5
  978.0 1445.7 %all-reduce.8.cloned.1.call-start = ((), (), s32[]{:S(2)}) async-start(), calls=%async_computation.2 | async-start | bytes 196608 | tf_op jit(solution)/shard_map/psum | solution.py:68
  2425.5 4.2 copy-start.2
  2425.5 4.2 copy-start.9
  2425.6 4.2 copy-start.11
  2429.7 21.0 copy-start.6
  2438.9 11.8 collective-permute-start
  2453.1 11.6 collective-permute-start.2
Sparse Core Ops, SparseCore 0:
  12.2 81.8 all-gather.6
  98.3 73.8 all-gather.8
  176.4 73.8 all-gather.10
  252.8 711.4 all-reduce.3
  978.1 714.9 all-reduce.5
  1708.7 714.9 all-reduce.7
where the time goes:
time: 2490 us; the launch traced here: 2480 us
  waiting for transfers between devices  2350 us (94%)
  matrix products  66.2 us (3%)
    psum x3, waiting for transfers between devices, shards(): lax.psum(kernel_apply(gathered, gathered_norms, records, work_norms, work...  2130 us
    all_gather x3, waiting for transfers between devices, shards(): gathered = lax.all_gather(records[local_rows], 'blk', axis=0, tiled=True)  202 us
  transfers between devices with their start and end apart: 9, of which 8 were waited for; matrix products, arithmetic and copies ran while one was open for 3% of the time, Pallas kernels for 0%

commit v1 on v0

--- a/solution.py
+++ b/solution.py
@@ -62,7 +62,10 @@
         local_rows = block_local[repeat]
         own_count = lax.dynamic_index_in_dim(block_count[repeat], own_index, 0, keepdims=False)
         is_live = slot_ids < own_count
-        gathered = lax.all_gather(records[local_rows], "blk", axis=0, tiled=True)
+        gathered = jnp.concatenate(
+            lax.all_to_all(jnp.stack([records[local_rows]] * lax.axis_size("blk")), "blk", 0, 0),
+            axis=0,
+        )
         gathered_norms = square_norms(gathered)
         work_coefs = coefficients
         whole_sum = lax.psum(

time: 2490 us -> 2400 us (0.964)
  waiting for transfers between devices: 2350 us -> 2230 us
  starting transfers between devices: 0.92 us -> 30.7 us
    all_gather x3 -> x0, waiting for transfers between devices: 202 us -> none  [shards(): gathered = lax.all_gather(records[local_rows], 'blk', axis=0, tiled=True)]
    all_to_all x0 -> x3, waiting for transfers between devices: none -> 86.5 us  [shards(): lax.all_to_all(jnp.stack([records[local_rows]] * lax.axis_size('blk')), '...]
    all_to_all x0 -> x3, starting transfers between devices: none -> 29.3 us  [shards(): lax.all_to_all(jnp.stack([records[local_rows]] * lax.axis_size('blk')), '...]
where the time goes in v1:
time: 2400 us; the launch traced here: 2390 us
  waiting for transfers between devices  2230 us (93%)
  matrix products  66.1 us (3%)
  starting transfers between devices  30.7 us (1%)
    psum x3, waiting for transfers between devices, shards(): lax.psum(kernel_apply(gathered, gathered_norms, records, work_norms, work...  2120 us
    all_to_all x3, waiting for transfers between devices, shards(): lax.all_to_all(jnp.stack([records[local_rows]] * lax.axis_size('blk')), '...  86.5 us
  transfers between devices with their start and end apart: 9, of which 8 were waited for; matrix products, arithmetic and copies ran while one was open for 3% of the time, Pallas kernels for 0%

profile of v1, /device:TPU:0, one launch (start us, length us, event | category | flops | bytes accessed | tf_op | source)
XLA Modules:
  0.0 2391.2 jit_solution(8808489701617389511)
XLA Ops:
  7.2 0.8 fusion.87
  8.0 2.0 gather_fusion
  10.0 1.2 stack.6
  11.2 13.1 all-to-all-start
  25.0 38.5 %all-to-all-done = bf16[64,24,512]{2,1,0:T(8,128)(2,1)} async-done(((bf16[64,24,512]{2,1,0:T(8,128)(2,1)}), bf16[64,24,512]{2,1,0:T(8,128)(2,1)}, u32[]{:S(2)}, u32[]{:S(2)}) %all-to-all-start) | async-done | bytes 1572896 | tf_op jit(solution)/shard_map/all_to_all | solution.py:66
  63.5 1.2 stack.7
  64.7 8.2 all-to-all-start.1
  76.5 1.0 copy.52
  77.7 35.2 %all-to-all-done.1 = bf16[64,24,512]{2,1,0:T(8,128)(2,1)} async-done(((bf16[64,24,512]{2,1,0:T(8,128)(2,1)}), bf16[64,24,512]{2,1,0:T(8,128)(2,1)}, u32[]{:S(2)}, u32[]{:S(2)}) %all-to-all-start.1) | async-done | bytes 1572896 | tf_op jit(solution)/shard_map/all_to_all | solution.py:66
  112.9 1.2 stack.8
  114.1 8.0 all-to-all-start.2
  124.4 0.7 iota_compare_fusion.1
  126.1 2.1 fusion.110
  128.2 2.0 fusion.109
  130.3 1.8 multiply_reduce_fusion.2
  132.2 3.3 fusion.106
  135.5 7.4 fusion.16
  143.5 5.9 fusion.107
  149.4 12.8 all-to-all-done.2
  162.2 5.9 fusion.108
  168.1 1.8 multiply_reduce_fusion.1
  169.9 698.1 %all-reduce.4.cloned.1.call-done = f32[1536,16]{0,1:T(8,128)} async-done(((f32[1536,16]{0,1:T(8,128)}), f32[1536,16]{0,1:T(8,128)}) %all-reduce.4.cloned.1.call-update) | async-done | bytes 98320 | tf_op jit(solution)/shard_map/psum | solution.py:71
  868.0 0.8 select_multiply_fusion.2
  868.9 2.5 scatter_fusion
  871.4 1.9 broadcast_multiply_fusion
  873.3 0.8 copy-done.6
  874.1 10.3 fusion.8
  884.5 1.8 multiply_reduce_fusion
  886.4 1.6 gather_fusion.4
  888.0 711.5 %all-reduce.6.cloned.1.call-done = f32[1536,16]{0,1:T(8,128)} async-done(((f32[1536,16]{0,1:T(8,128)}), f32[1536,16]{0,1:T(8,128)}) %all-reduce.6.cloned.1.call-update) | async-done | bytes 98320 | tf_op jit(solution)/shard_map/psum | solution.py:71
  1599.6 0.8 select_multiply_fusion.1
  1600.4 2.7 scatter_fusion.1
  1603.1 1.3 broadcast_multiply_fusion.1
  1604.4 0.8 copy-done.4
  1605.2 10.3 fusion
  1615.5 3.2 fusion.111
  1619.4 711.3 %all-reduce.8.cloned.1.call-done = f32[1536,16]{0,1:T(8,128)} async-done(((f32[1536,16]{0,1:T(8,128)}), f32[1536,16]{0,1:T(8,128)}) %all-reduce.8.cloned.1.call-update) | async-done | bytes 98320 | tf_op jit(solution)/shard_map/psum | solution.py:71
  2330.7 0.8 select_multiply_fusion
  2331.5 0.9 scatter_fusion.2
  2332.5 4.1 fusion.63
  2336.7 9.1 fusion.60
  2346.2 1.2 multiply_reduce_fusion.4
  2347.4 10.3 collective-permute-done
  2357.7 2.4 fusion.69
  2360.2 0.8 copy.63
  2361.0 0.8 copy.64
  2361.8 9.9 collective-permute-done.2
  2371.7 11.5 psum.31
  (71 shorter events, 11.1 us)
Async XLA Ops:
  7.2 121.1 %copy-start = (bf16[512,1024]{1,0:T(8,128)(2,1)S(1)}, bf16[512,1024]{1,0:T(8,128)(2,1)}, u32[]{:S(2)}) copy-start(bf16[512,1024]{1,0:T(8,128)(2,1)} %param.17) | copy-start | bytes 3145732
  10.0 14.4 copy-start.1
  11.2 52.3 %all-to-all-start = ((bf16[64,24,512]{2,1,0:T(8,128)(2,1)}), bf16[64,24,512]{2,1,0:T(8,128)(2,1)}, u32[]{:S(2)}, u32[]{:S(2)}) async-start(bf16[64,24,512]{2,1,0:T(8,128)(2,1)} %stack.6), calls=%async_computation | async-start | bytes 3145728 | tf_op jit(solution)/shard_map/all_to_all | solution.py:66
  25.0 47.9 %copy-start.3 = (bf16[512,512]{1,0:T(8,128)(2,1)S(1)}, bf16[512,512]{1,0:T(8,128)(2,1)}, u32[]{:S(2)}) copy-start(bf16[512,512]{1,0:T(8,128)(2,1)} %param.16) | copy-start | bytes 1572868
  25.0 48.0 %copy-start.8 = (f32[1024,16]{0,1:T(8,128)S(1)}, f32[1024,16]{0,1:T(8,128)}, u32[]{:S(2)}) copy-start(f32[1024,16]{0,1:T(8,128)} %param.13) | copy-start | bytes 196612
  64.7 10.9 copy-start.9
  64.7 11.7 copy-start.11
  64.7 48.1 %all-to-all-start.1 = ((bf16[64,24,512]{2,1,0:T(8,128)(2,1)}), bf16[64,24,512]{2,1,0:T(8,128)(2,1)}, u32[]{:S(2)}, u32[]{:S(2)}) async-start(bf16[64,24,512]{2,1,0:T(8,128)(2,1)} %stack.7), calls=%async_computation.1 | async-start | bytes 3145728 | tf_op jit(solution)/shard_map/all_to_all | solution.py:66
  72.9 1542.6 %collective-permute-start.1 = (bf16[512,512]{1,0:T(8,128)(2,1)S(1)}, bf16[512,512]{1,0:T(8,128)(2,1)}, u32[]{:S(2)}, u32[]{:S(2)}) collective-permute-start(bf16[512,512]{1,0:T(8,128)(2,1)S(1)} %copy-done.3), channel_id=1, source_target_pairs={{0,4},{4,8},{8,12},{12,16},{16,20},{20,24},{24,28},{28,32},{32,36}... | collective-permute-start | bytes 1572872 | tf_op jit(solution)/shard_map/ppermute | solution.py:16
  77.6 44.9 %copy-start.13 = (s32[3,64]{1,0:T(4,128)S(1)}, s32[3,64]{1,0:T(4,128)}, u32[]{:S(2)}) copy-start(s32[3,64]{1,0:T(4,128)} %param.15) | copy-start | bytes 2308
  114.1 48.0 %all-to-all-start.2 = ((bf16[64,24,512]{2,1,0:T(8,128)(2,1)}), bf16[64,24,512]{2,1,0:T(8,128)(2,1)}, u32[]{:S(2)}, u32[]{:S(2)}) async-start(bf16[64,24,512]{2,1,0:T(8,128)(2,1)} %stack.8), calls=%async_computation.2 | async-start | bytes 3145728 | tf_op jit(solution)/shard_map/all_to_all | solution.py:66
  122.2 745.8 %all-reduce.4.cloned.1.call-start = ((), (), s32[]{:S(2)}) async-start(), calls=%async_computation.3 | async-start | bytes 196608 | tf_op jit(solution)/shard_map/psum | solution.py:71
  142.9 1456.7 %all-reduce.6.cloned.1.call-start = ((), (), s32[]{:S(2)}) async-start(), calls=%async_computation.4 | async-start | bytes 196608 | tf_op jit(solution)/shard_map/psum | solution.py:71
  873.3 0.8 copy-start.6
  884.4 1446.2 %all-reduce.8.cloned.1.call-start = ((), (), s32[]{:S(2)}) async-start(), calls=%async_computation.5 | async-start | bytes 196608 | tf_op jit(solution)/shard_map/psum | solution.py:71
  1604.4 0.8 copy-start.4
  1615.5 3.2 copy-start.5
  2332.5 4.2 copy-start.2
  2332.5 4.2 copy-start.10
  2332.5 4.2 copy-start.12
  2336.7 21.0 copy-start.7
  2345.9 11.9 collective-permute-start
  2360.1 11.6 collective-permute-start.2
Sparse Core Ops, SparseCore 0:
  143.0 724.9 all-reduce.3
  884.6 714.9 all-reduce.5
  1615.6 714.9 all-reduce.7
